TPU v7x, 32 devices: a whole 2x2x4 slice. The times are simulated.
32 devices in a mesh: front: 8 (over z, x), grp: 4 (over y, core).
Axes of the slice: x: 2, y: 2, z: 4, core: 2. Of those that a mesh axis runs over, the one named last changes fastest.
Arguments:
- front_block: float32 [8, 16384, 1408], P('front', 'grp'), as said below
- child_blocks: float32 [8, 4, 4, 16, 1408], P('front', 'grp'), may hold values from -0.5 to 0.5
- child_rows: int32 [8, 4, 4, 16], P('front', 'grp'), may hold values from 0 to 4095
- child_dest: int32 [8, 4, 4, 1], P('front', 'grp'), may hold values from 0 to 7; in each aligned block of 4 rows (0 to 3, 4 to 7, ..., all dimensions but the last counted through in order) at most 2 rows name the same one
- panel_owner: int32 [8], P('front'), may hold values from 0 to 3
Outputs:
- panel_factor: float32 [8, 16384, 512], P('front', 'grp')
- schur_block: float32 [8, 16384, 896], P('front', 'grp')
Inputs may be any that keep to these rules, and one draw needn't show every extreme that they name: `child_dest`: among the 4 blocks of one device no front is named more than 2 times, and in every draw some device names some front exactly 2 times. `front_block`: for every front and row block, the first 512 rows' leading 512 x 512 block has a positive diagonal that dominates; other entries lie within -2.3 to 2.3.
All inputs are finite; a program needn't handle non-finite values.
Results may differ from a plain program's by a relative error of at most 0.0003.
Values sent between devices are 32-bit elements; how exact they have to be, the bound alone decides.
No kernel may reach another device: no remote copies, remote signals or barrier semaphores. Data moves between devices by JAX's collectives and lax.ppermute only.
A program may use at most 128 MiB of HBM per device.

v0:
```python
import jax
import jax.numpy as jnp
from jax import lax
from jax.sharding import PartitionSpec as P

PB = 512
CAP = 2


def spread(array, axis, root):
    mine = lax.axis_index(axis) == root
    return lax.psum(jnp.where(mine, array, jnp.zeros_like(array)), axis)


def right_solve(factor, rows):
    return lax.linalg.triangular_solve(factor, rows, left_side=False, lower=True, transpose_a=True)


def pack_slots(values, slot_index, front_count):
    empty = jnp.zeros((front_count * CAP,) + values.shape[1:], values.dtype)
    filled = empty.at[slot_index].set(values)
    return filled.reshape((front_count, CAP) + values.shape[1:])


def local(front_block, child_blocks, child_rows, child_dest, panel_owner):
    local_rows = front_block[0]
    front_count = lax.axis_size("front")
    blocks = child_blocks[0, 0]
    row_lists = child_rows[0, 0]
    target_front = child_dest[0, 0, :, 0]
    block_count = target_front.shape[0]
    position = jnp.arange(block_count, dtype=jnp.int32)
    same_front = target_front[:, None] == target_front[None, :]
    earlier = position[None, :] < position[:, None]
    slot_index = target_front * CAP + jnp.sum((same_front & earlier).astype(jnp.int32), axis=1)
    send_rows = pack_slots(row_lists, slot_index, front_count)
    panel_cols = PB
    send_panel = pack_slots(blocks[:, :, :panel_cols], slot_index, front_count)
    got_panel, got_rows = (
        lax.all_to_all(send_panel, "front", split_axis=0, concat_axis=0, tiled=True),
        lax.all_to_all(send_rows, "front", split_axis=0, concat_axis=0, tiled=True),
    )
    flat_rows = got_rows.reshape(-1)
    panel_part = local_rows[:, :panel_cols].at[flat_rows].add(got_panel.reshape(-1, panel_cols))
    local_rows = jnp.concatenate([panel_part, local_rows[:, panel_cols:]], axis=1)
    send_trail = pack_slots(blocks[:, :, panel_cols:], slot_index, front_count)
    trailing_rows = lax.all_to_all(send_trail, "front", split_axis=0, concat_axis=0, tiled=True)
    win_cols = local_rows.shape[1] - panel_cols
    owner_index = panel_owner[0]
    is_owner = lax.axis_index("grp") == owner_index
    pivot_block = spread(local_rows[:panel_cols, :panel_cols], "grp", owner_index)
    symmetric = 0.5 * (pivot_block + pivot_block.T)
    pivot_factor = jnp.linalg.cholesky(symmetric)
    solved = right_solve(pivot_factor, local_rows[:, :panel_cols])
    window = spread(solved[panel_cols : panel_cols + win_cols], "grp", owner_index)
    schur_part = local_rows[:, panel_cols:] - jnp.dot(
        solved, window.T, precision=lax.Precision.HIGHEST
    )
    schur_part = schur_part.at[flat_rows].add(trailing_rows.reshape(-1, win_cols))
    top_rows = jnp.where(is_owner, pivot_factor, solved[:panel_cols])
    panel_rows = jnp.concatenate([top_rows, solved[panel_cols:]], axis=0)
    return (panel_rows[None], schur_part[None])


def solution(mesh):
    placed = (
        P("front", "grp", None),
        P("front", "grp", None, None, None),
        P("front", "grp", None, None),
        P("front", "grp", None, None),
        P("front"),
    )
    return jax.shard_map(
        local,
        mesh=mesh,
        in_specs=placed,
        out_specs=(P("front", "grp", None), P("front", "grp", None)),
        check_vma=False,
    )
```

profile of v0, /device:TPU:0, one launch (start us, length us, event | category | flops | bytes accessed | tf_op | source)
XLA Modules:
  0.0 376.9 jit_solution(13516703856548817198)
XLA Ops:
  7.2 0.9 convert_reduce_fusion
  8.1 0.7 fusion.38
  8.8 1.2 scatter_custom_fusion
  9.9 7.3 %all-to-all-start = ((s32[8,2,16]{2,1,0:T(2,128)}), s32[8,2,16]{2,1,0:T(2,128)S(1)}, u32[]{:S(2)}, u32[]{:S(2)}) async-start(s32[8,2,16]{2,1,0:T(2,128)} %bitcast.7), calls=%async_computation | async-start | bytes 16384 | tf_op jit(solution)/shard_map/all_to_all | solution.py:41
  17.2 0.9 slice.147
  18.1 0.9 broadcast_in_dim.31
  18.9 2.0 scatter_fusion
  21.0 2.7 all-to-all-done
  23.7 3.5 all-to-all-start.1
  27.9 7.9 %slice.146 = f32[4096,512]{1,0:T(8,128)} slice(f32[4096,1408]{1,0:T(8,128)} %bitcast.80), slice={[0:4096], [0:512]} | slice | bytes 16777216 | tf_op jit(solution)/shard_map/slice | solution.py:44
  35.9 5.0 %all-to-all-done.1 = f32[8,2,16,512]{3,2,1,0:T(8,128)S(1)} async-done(((f32[8,2,16,512]{3,2,1,0:T(8,128)}), f32[8,2,16,512]{3,2,1,0:T(8,128)S(1)}, u32[]{:S(2)}, u32[]{:S(2)}) %all-to-all-start.1) | async-done | bytes 524320 | tf_op jit(solution)/shard_map/all_to_all | solution.py:40
  40.9 9.0 %scatter_fusion.1 = f32[4096,512]{1,0:T(8,128)} fusion(f32[4096,512]{1,0:T(8,128)} %slice.146, s32[256]{0:T(256)S(1)} %bitcast.85, f32[256,512]{1,0:T(8,128)S(1)} %bitcast.82), kind=kCustom, calls=%fused_computation.2 | custom fusion | flops 131072 | bytes 1573888 | tf_op jit(solution)/shard_map/scatter-add | solution.py:44
  49.9 1.3 slice.148
  51.6 1.1 broadcast_select_fusion
  52.7 1.0 broadcast_in_dim.35
  53.7 2.2 scatter_fusion.2
  55.9 4.2 %all-to-all-start.2 = ((f32[8,2,16,896]{3,2,1,0:T(8,128)}), f32[8,2,16,896]{3,2,1,0:T(8,128)}, u32[]{:S(2)}, u32[]{:S(2)}) async-start(f32[8,2,16,896]{3,2,1,0:T(8,128)} %bitcast.25), calls=%async_computation.2 | async-start | bytes 1835008 | tf_op jit(solution)/shard_map/all_to_all | solution.py:47
  60.7 27.5 %all-reduce.4.cloned.1.call-done = f32[512,512]{0,1:T(8,128)} async-done(((f32[512,512]{0,1:T(8,128)}), f32[512,512]{0,1:T(8,128)}) %all-reduce.4.cloned.1.call-update) | async-done | bytes 1048592 | tf_op jit(solution)/shard_map/psum | solution.py:12
  88.1 1.6 copy.34
  90.6 11.7 %cholesky.103 = f32[128,128]{1,0:T(8,128)S(1)} custom-call(f32[128,128]{1,0:T(8,128)S(1)} %cholesky.263), custom_call_target="Cholesky" | custom-call | tf_op jit(solution)/shard_map/jit(cholesky)/cholesky | solution.py:53
  102.5 9.8 %custom-call.30 = f32[1,128,128]{1,2,0:T(8,128)S(1)} custom-call(f32[1,128,128]{2,1,0:T(8,128)S(1)} %get-tuple-element.43), custom_call_target="InvertDiagBlocksLowerTriangular" | custom-call | tf_op jit(solution)/shard_map/jit(cholesky)/cholesky | solution.py:53
  113.1 11.7 %cholesky.215 = f32[128,128]{1,0:T(8,128)S(1)} custom-call(f32[128,128]{1,0:T(8,128)S(1)} %cholesky.267), custom_call_target="Cholesky" | custom-call | tf_op jit(solution)/shard_map/jit(cholesky)/cholesky | solution.py:53
  125.0 9.9 %custom-call.31 = f32[1,128,128]{1,2,0:T(8,128)S(1)} custom-call(f32[1,128,128]{2,1,0:T(8,128)S(1)} %get-tuple-element.41), custom_call_target="InvertDiagBlocksLowerTriangular" | custom-call | tf_op jit(solution)/shard_map/jit(cholesky)/cholesky | solution.py:53
  135.4 1.5 convolution_subtract_fusion.3
  136.9 11.7 %cholesky.236 = f32[128,128]{1,0:T(8,128)S(1)} custom-call(f32[128,128]{1,0:T(8,128)S(1)} %cholesky.272), custom_call_target="Cholesky" | custom-call | tf_op jit(solution)/shard_map/jit(cholesky)/cholesky | solution.py:53
  148.8 9.8 %custom-call.32 = f32[1,128,128]{1,2,0:T(8,128)S(1)} custom-call(f32[1,128,128]{2,1,0:T(8,128)S(1)} %get-tuple-element.39), custom_call_target="InvertDiagBlocksLowerTriangular" | custom-call | tf_op jit(solution)/shard_map/jit(cholesky)/cholesky | solution.py:53
  158.9 1.3 convolution_subtract_fusion.4
  160.2 12.1 %cholesky.253 = f32[128,128]{1,0:T(8,128)S(1)} custom-call(f32[128,128]{1,0:T(8,128)S(1)} %convolution_subtract_fusion.4), custom_call_target="Cholesky" | custom-call | tf_op jit(solution)/shard_map/jit(cholesky)/cholesky | solution.py:53
  172.4 0.7 compare_reduce_fusion.1
  173.2 0.6 compare_reduce_fusion
  173.8 0.7 compare_reduce_fusion.2
  177.1 11.3 %while.1 = (s32[]{:T(128)}, f32[512,512]{0,1:T(8,128)S(1)}, s32[4,2]{0,1:T(2,128)S(1)}, f32[4,128,128]{2,1,0:T(8,128)}, s32[]{:T(128)}) while((s32[]{:T(128)}, f32[512,512]{0,1:T(8,128)S(1)}, s32[4,2]{0,1:T(2,128)S(1)}, f32[4,128,128]{2,1,0:T(8,128)}, s32[]{:T(128)}) %tuple.33), condition=%wide.while_cond, body=%wide.while_body.sunk | while | flops 2 | bytes 393329 | solution.py:16
  177.2 0.6 fusion.49
  177.8 1.4 dynamic-slice.7
  179.4 0.6 bitcast_dynamic-update-slice_fusion.2
  180.1 0.6 fusion.49
  180.7 1.4 dynamic-slice.7
  182.2 0.6 bitcast_dynamic-update-slice_fusion.2
  183.5 1.4 dynamic-slice.7
  185.0 0.6 bitcast_dynamic-update-slice_fusion.2
  185.7 0.6 fusion.49
  186.3 1.4 dynamic-slice.7
  187.8 0.6 bitcast_dynamic-update-slice_fusion.2
  188.5 1.0 copy-done.9
  189.4 40.1 %custom-call.33 = f32[4,128,128]{1,2,0:T(8,128)S(1)} custom-call(f32[4,128,128]{2,1,0:T(8,128)} %get-tuple-element.9), custom_call_target="InvertDiagBlocksLowerTriangular" | custom-call | tf_op jit(solution)/shard_map/triangular_solve | solution.py:16
  229.6 3.6 fusion.12
  233.2 5.2 %convolution_subtract_fusion.1 = f32[4096,128]{1,0:T(8,128)S(1)} fusion(f32[4096,128]{0,1:T(8,128)S(1)} %fusion.12, f32[4096,512]{1,0:T(8,128)} %scatter_fusion.1, f32[512,512]{0,1:T(8,128)} %copy-done.9), kind=kOutput, calls=%fused_computation.17 | convolution fusion | flops 805830656 | bytes 6356992 | tf_op jit(solution)/shard_map/triangular_solve | solution.py:16
  238.4 2.0 fusion.27
  240.4 9.8 %convolution_subtract_fusion = f32[4096,128]{1,0:T(8,128)S(1)} fusion(f32[4096,128]{0,1:T(8,128)S(1)} %fusion.27, f32[4096,128]{0,1:T(8,128)S(1)} %fusion.12, f32[4096,512]{1,0:T(8,128)} %scatter_fusion.1, f32[512,512]{0,1:T(8,128)} %copy-done.9), kind=kOutput, calls=%fused_computation.16 | convolution fusion | flops 1612185600 | bytes 8519680 | tf_op jit(solution)/shard_map/triangular_solve | solution.py:16
  250.2 2.0 fusion.26
  252.2 12.8 %fusion.6 = f32[4096,128]{1,0:T(8,128)S(1)} fusion(f32[4096,128]{0,1:T(8,128)S(1)} %fusion.26, f32[4096,128]{0,1:T(8,128)S(1)} %fusion.27, f32[4096,128]{0,1:T(8,128)S(1)} %fusion.12, f32[4096,512]{1,0:T(8,128)} %scatter_fusion.1, f32[512,512]{0,1:T(8,128)} %copy-done.9), kind=kOutput, calls=%fused_computation.18 | convolution fusion | flops 2419589120 | bytes 10682368 | tf_op jit(solution)/shard_map/triangular_solve | solution.py:16
  265.0 2.1 fusion.25
  267.1 1.3 copy-done.6
  268.5 1.5 maximum_select_fusion
  270.0 5.9 %pad_maximum_fusion = f32[4096,512]{0,1:T(8,128)} fusion(f32[4096,128]{0,1:T(8,128)} %copy-done.6, f32[4096,128]{0,1:T(8,128)} %copy-done.4, f32[4096,128]{0,1:T(8,128)} %copy-done.2, f32[4096,128]{0,1:T(8,128)S(1)} %fusion.12), kind=kLoop, calls=%fused_computation.8 | loop fusion | flops 6291456 | bytes 16777216 | tf_op jit(solution)/shard_map/triangular_solve | solution.py:16
  275.9 1.6 copy-done.3
  277.5 0.6 copy-done.5
  278.1 0.6 copy-done.7
  278.9 3.1 slice-done
  282.0 3.9 %maximum_bitcast_fusion = f32[1,4096,512]{1,2,0:T(8,128)} fusion(f32[3584,512]{0,1:T(8,128)S(1)} %slice-done, f32[512,512]{0,1:T(8,128)S(1)} %maximum_select_fusion.1), kind=kLoop, calls=%fused_computation.9 | loop fusion | flops 2097152 | bytes 16777216 | tf_op jit(solution)/shard_map/broadcast_in_dim | solution.py:62
  285.9 9.0 %copy.44 = f32[1,4096,512]{2,1,0:T(8,128)} copy(f32[1,4096,512]{1,2,0:T(8,128)} %maximum_bitcast_fusion) | data formatting | bytes 16777216
  294.9 28.4 %all-reduce.6.cloned.1.call-done = f32[896,512]{0,1:T(8,128)} async-done(((f32[896,512]{0,1:T(8,128)}), f32[896,512]{0,1:T(8,128)}) %all-reduce.6.cloned.1.call-update) | async-done | bytes 1835024 | tf_op jit(solution)/shard_map/psum | solution.py:12
  323.3 32.7 %slice_subtract_fusion = f32[4096,896]{1,0:T(8,128)} fusion(f32[4096,1408]{1,0:T(8,128)} %bitcast.81, f32[896,512]{0,1:T(8,128)} %all-reduce.6.cloned.1.call-done, f32[4096,128]{0,1:T(8,128)} %copy-done.6, f32[4096,128]{0,1:T(8,128)} %copy-done.4, f32[4096,128]{0,1:T(8,128)} %copy-done.2, f32[4096,128]{0,1:T(8,128)S(1)} %fusion.12), kind=kOutput, calls=%fused_computation.7 | convolution fusion | flops 22558539776 | bytes 39583744 | tf_op jit(solution)/shard_map/dot_general | solution.py:56
  356.0 13.9 %scatter_fusion.3 = f32[4096,896]{1,0:T(8,128)} fusion(f32[4096,896]{1,0:T(8,128)} %slice_subtract_fusion, s32[256]{0:T(256)S(1)} %bitcast.86, f32[256,896]{1,0:T(8,128)} %bitcast.26), kind=kCustom, calls=%fused_computation.4 | custom fusion | flops 229376 | bytes 2753536 | tf_op jit(solution)/shard_map/scatter-add | solution.py:59
  (67 shorter events, 5.5 us)
Async XLA Ops:
  7.2 1.6 copy-start
  9.9 13.8 %all-to-all-start = ((s32[8,2,16]{2,1,0:T(2,128)}), s32[8,2,16]{2,1,0:T(2,128)S(1)}, u32[]{:S(2)}, u32[]{:S(2)}) async-start(s32[8,2,16]{2,1,0:T(2,128)} %bitcast.7), calls=%async_computation | async-start | bytes 16384 | tf_op jit(solution)/shard_map/all_to_all | solution.py:41
  23.7 17.2 %all-to-all-start.1 = ((f32[8,2,16,512]{3,2,1,0:T(8,128)}), f32[8,2,16,512]{3,2,1,0:T(8,128)S(1)}, u32[]{:S(2)}, u32[]{:S(2)}) async-start(f32[8,2,16,512]{3,2,1,0:T(8,128)} %bitcast.10), calls=%async_computation.1 | async-start | bytes 1048576 | tf_op jit(solution)/shard_map/all_to_all | solution.py:40
  27.2 61.0 %all-reduce.4.cloned.1.call-start = ((), (), s32[]{:S(2)}) async-start(), calls=%async_computation.3 | async-start | bytes 2097152 | tf_op jit(solution)/shard_map/psum | solution.py:12
  51.6 1.1 copy-start.11
  55.9 300.1 %all-to-all-start.2 = ((f32[8,2,16,896]{3,2,1,0:T(8,128)}), f32[8,2,16,896]{3,2,1,0:T(8,128)}, u32[]{:S(2)}, u32[]{:S(2)}) async-start(f32[8,2,16,896]{3,2,1,0:T(8,128)} %bitcast.25), calls=%async_computation.2 | async-start | bytes 1835008 | tf_op jit(solution)/shard_map/all_to_all | solution.py:47
  60.1 263.2 %all-reduce.6.cloned.1.call-start = ((), (), s32[]{:S(2)}) async-start(), calls=%async_computation.4 | async-start | bytes 3670016 | tf_op jit(solution)/shard_map/psum | solution.py:12
  88.1 1.7 copy-start.8
  90.6 34.4 %copy-start.10 = (f32[512,512]{1,0:T(8,128)}, f32[512,512]{1,0:T(8,128)S(1)}, u32[]{:S(2)}) copy-start(f32[512,512]{1,0:T(8,128)S(1)} %fusion.14) | copy-start | bytes 3145732
  188.5 1.0 copy-start.9
  240.4 26.7 %copy-start.2 = (f32[4096,128]{0,1:T(8,128)}, f32[4096,128]{0,1:T(8,128)S(1)}, u32[]{:S(2)}) copy-start(f32[4096,128]{0,1:T(8,128)S(1)} %fusion.27) | copy-start | bytes 6291460
  252.2 14.9 %copy-start.4 = (f32[4096,128]{0,1:T(8,128)}, f32[4096,128]{0,1:T(8,128)S(1)}, u32[]{:S(2)}) copy-start(f32[4096,128]{0,1:T(8,128)S(1)} %fusion.26) | copy-start | bytes 6291460
  267.1 1.4 copy-start.6
  275.9 1.6 copy-start.3
  275.9 2.2 copy-start.5
  275.9 2.8 copy-start.7
  278.7 3.3 slice-start
  356.0 13.9 %copy-start.1 = (s32[1,1,4,16]{3,2,1,0:T(4,128)S(1)}, s32[1,1,4,16]{3,2,1,0:T(4,128)}, u32[]{:S(2)}) copy-start(s32[1,1,4,16]{3,2,1,0:T(4,128)} %param.7) | copy-start | bytes 772
Sparse Core Ops, SparseCore 0:
  52.8 35.3 all-reduce.3
  276.0 47.2 all-reduce.5
where the time goes:
time: 382 us; the launch traced here: 377 us
  other arithmetic  157 us (41%)
  matrix products  74.2 us (19%)
  waiting for transfers between devices  63.7 us (17%)
  local copies, waits for them, and re-layouts  48.9 us (13%)
  between operations  17.9 us (5%)
  starting transfers between devices  15.5 us (4%)
    another operation x14, other arithmetic, local(): pivot_factor = jnp.linalg.cholesky(symmetric)  78.9 us
    psum x2, waiting for transfers between devices, spread(): return lax.psum(jnp.where(mine, array, jnp.zeros_like(array)), axis)  55.9 us
    another operation x4, other arithmetic, right_solve(): lax.linalg.triangular_solve(factor, rows, left_side=False, lower=True, tr...  46.2 us
    another operation x7, matrix products, right_solve(): lax.linalg.triangular_solve(factor, rows, left_side=False, lower=True, tr...  37.5 us
    dot_general x1, matrix products, local(): jnp.dot(solved, window.T, precision=lax.Precision.HIGHEST)  32.7 us
    unnamed x26, local copies, waits for them, and re-layouts  14.5 us
    scatter-add x1, other arithmetic, local(): schur_part.at[flat_rows].add(trailing_rows.reshape(-1, win_cols))  13.9 us
    another operation x20, local copies, waits for them, and re-layouts  11.2 us
  transfers between devices with their start and end apart: 5, of which 4 were waited for; matrix products, arithmetic and copies ran while one was open for 65% of the time, Pallas kernels for 0%

commit v1 on v0

--- a/solution.py
+++ b/solution.py
@@ -9,7 +9,7 @@
 
 def spread(array, axis, root):
     mine = lax.axis_index(axis) == root
-    return lax.psum(jnp.where(mine, array, jnp.zeros_like(array)), axis)
+    return jnp.sum(lax.all_gather(jnp.where(mine, array, jnp.zeros_like(array)), axis), axis=0)
 
 
 def right_solve(factor, rows):

time: 382 us -> 398 us (1.042)
  waiting for transfers between devices: 63.7 us -> 72.2 us
  other arithmetic: 157 us -> 165 us
  local copies, waits for them, and re-layouts: 48.9 us -> 43.4 us
  matrix products: 74.2 us -> 78.3 us
    all_gather x0 -> x2, waiting for transfers between devices: none -> 64.2 us  [spread(): lax.all_gather(jnp.where(mine, array, jnp.zeros_like(array)), axis)]
    psum x2 -> x0, waiting for transfers between devices: 55.9 us -> none  [spread(): return lax.psum(jnp.where(mine, array, jnp.zeros_like(array)), axis)]
    reduce_sum x0 -> x2, other arithmetic: none -> 8.22 us  [spread(): jnp.sum(lax.all_gather(jnp.where(mine, array, jnp.zeros_like(array)), axi...]
    another operation x1 -> x4, local copies, waits for them, and re-layouts: 0.01 us -> 8.11 us  [right_solve(): lax.linalg.triangular_solve(factor, rows, left_side=False, lower=True, tr...]
    unnamed x26 -> x24, local copies, waits for them, and re-layouts: 14.5 us -> 6.62 us
    another operation x20 -> x12, local copies, waits for them, and re-layouts: 11.2 us -> 10.3 us
  transfers between devices with their start and end apart: 5 -> 5, of which waited for: 4 -> 4; matrix products, arithmetic and copies ran while one was open for 65% -> 16% of each run, Pallas kernels for 0% -> 0%
where the time goes in v1:
time: 398 us; the launch traced here: 394 us
  other arithmetic  165 us (41%)
  matrix products  78.3 us (20%)
  waiting for transfers between devices  72.2 us (18%)
  local copies, waits for them, and re-layouts  43.4 us (11%)
  between operations  17.8 us (4%)
  starting transfers between devices  17.1 us (4%)
    another operation x14, other arithmetic, local(): pivot_factor = jnp.linalg.cholesky(symmetric)  78.8 us
    all_gather x2, waiting for transfers between devices, spread(): lax.all_gather(jnp.where(mine, array, jnp.zeros_like(array)), axis)  64.2 us
    another operation x4, other arithmetic, right_solve(): lax.linalg.triangular_solve(factor, rows, left_side=False, lower=True, tr...  44.3 us
    another operation x7, matrix products, right_solve(): lax.linalg.triangular_solve(factor, rows, left_side=False, lower=True, tr...  39.9 us
    dot_general x1, matrix products, local(): jnp.dot(solved, window.T, precision=lax.Precision.HIGHEST)  32.9 us
    scatter-add x1, other arithmetic, local(): schur_part.at[flat_rows].add(trailing_rows.reshape(-1, win_cols))  13.9 us
    another operation x12, local copies, waits for them, and re-layouts  10.3 us
    scatter-add x1, other arithmetic, local(): local_rows[:, :panel_cols].at[flat_rows]  9.01 us
  transfers between devices with their start and end apart: 5, of which 4 were waited for; matrix products, arithmetic and copies ran while one was open for 16% of the time, Pallas kernels for 0%

profile of v1, /device:TPU:0, one launch (start us, length us, event | category | flops | bytes accessed | tf_op | source)
XLA Modules:
  0.0 393.9 jit_solution(2138249554151324940)
XLA Ops:
  7.2 0.9 convert_reduce_fusion
  8.1 0.7 fusion.38
  8.8 1.2 scatter_custom_fusion
  9.9 7.3 %all-to-all-start = ((s32[8,2,16]{2,1,0:T(2,128)}), s32[8,2,16]{2,1,0:T(2,128)S(1)}, u32[]{:S(2)}, u32[]{:S(2)}) async-start(s32[8,2,16]{2,1,0:T(2,128)} %bitcast.7), calls=%async_computation | async-start | bytes 16384 | tf_op jit(solution)/shard_map/all_to_all | solution.py:41
  17.2 0.9 slice.147
  18.1 0.9 broadcast_in_dim.31
  18.9 2.0 scatter_fusion
  21.0 2.7 all-to-all-done
  23.7 3.5 all-to-all-start.1
  27.9 7.8 %slice.146 = f32[4096,512]{1,0:T(8,128)} slice(f32[4096,1408]{1,0:T(8,128)} %bitcast.82), slice={[0:4096], [0:512]} | slice | bytes 16777216 | tf_op jit(solution)/shard_map/slice | solution.py:44
  35.7 5.2 %all-to-all-done.1 = f32[8,2,16,512]{3,2,1,0:T(8,128)S(1)} async-done(((f32[8,2,16,512]{3,2,1,0:T(8,128)}), f32[8,2,16,512]{3,2,1,0:T(8,128)S(1)}, u32[]{:S(2)}, u32[]{:S(2)}) %all-to-all-start.1) | async-done | bytes 524320 | tf_op jit(solution)/shard_map/all_to_all | solution.py:40
  40.9 9.0 %scatter_fusion.1 = f32[4096,512]{1,0:T(8,128)} fusion(f32[4096,512]{1,0:T(8,128)} %slice.146, s32[256]{0:T(256)S(1)} %bitcast.90, f32[256,512]{1,0:T(8,128)S(1)} %bitcast.87), kind=kCustom, calls=%fused_computation.2 | custom fusion | flops 131072 | bytes 1573888 | tf_op jit(solution)/shard_map/scatter-add | solution.py:44
  49.9 2.3 slice_select_fusion
  52.8 33.1 %all-gather.5.cloned.1.call-done = f32[2048,512]{1,0:T(8,128)} async-done(((f32[512,512]{1,0:T(8,128)}), f32[2048,512]{1,0:T(8,128)}) %all-gather.5.cloned.1.call-update) | async-done | bytes 4194320 | tf_op jit(solution)/shard_map/all_gather | solution.py:12
  85.9 2.8 reduce_sum.31
  89.3 1.0 copy-done.11
  90.3 11.7 %cholesky.103 = f32[128,128]{1,0:T(8,128)S(1)} custom-call(f32[128,128]{1,0:T(8,128)S(1)} %cholesky.263), custom_call_target="Cholesky" | custom-call | tf_op jit(solution)/shard_map/jit(cholesky)/cholesky | solution.py:53
  102.2 9.8 %custom-call.30 = f32[1,128,128]{1,2,0:T(8,128)S(1)} custom-call(f32[1,128,128]{2,1,0:T(8,128)S(1)} %get-tuple-element.29), custom_call_target="InvertDiagBlocksLowerTriangular" | custom-call | tf_op jit(solution)/shard_map/jit(cholesky)/cholesky | solution.py:53
  112.0 1.2 constant_dynamic-update-slice_fusion.3
  113.2 1.3 convolution_subtract_fusion.2
  114.5 11.7 %cholesky.215 = f32[128,128]{1,0:T(8,128)S(1)} custom-call(f32[128,128]{1,0:T(8,128)S(1)} %cholesky.267), custom_call_target="Cholesky" | custom-call | tf_op jit(solution)/shard_map/jit(cholesky)/cholesky | solution.py:53
  126.3 9.9 %custom-call.31 = f32[1,128,128]{1,2,0:T(8,128)S(1)} custom-call(f32[1,128,128]{2,1,0:T(8,128)S(1)} %get-tuple-element.26), custom_call_target="InvertDiagBlocksLowerTriangular" | custom-call | tf_op jit(solution)/shard_map/jit(cholesky)/cholesky | solution.py:53
  136.5 1.3 convolution_subtract_fusion.3
  137.8 11.7 %cholesky.236 = f32[128,128]{1,0:T(8,128)S(1)} custom-call(f32[128,128]{1,0:T(8,128)S(1)} %cholesky.272), custom_call_target="Cholesky" | custom-call | tf_op jit(solution)/shard_map/jit(cholesky)/cholesky | solution.py:53
  149.5 0.7 compare_reduce_fusion.1
  150.2 9.8 %custom-call.32 = f32[1,128,128]{1,2,0:T(8,128)S(1)} custom-call(f32[1,128,128]{2,1,0:T(8,128)S(1)} %get-tuple-element.23), custom_call_target="InvertDiagBlocksLowerTriangular" | custom-call | tf_op jit(solution)/shard_map/jit(cholesky)/cholesky | solution.py:53
  160.2 1.2 convolution_subtract_fusion.4
  161.5 11.9 %cholesky.253 = f32[128,128]{1,0:T(8,128)S(1)} custom-call(f32[128,128]{1,0:T(8,128)S(1)} %convolution_subtract_fusion.4), custom_call_target="Cholesky" | custom-call | tf_op jit(solution)/shard_map/jit(cholesky)/cholesky | solution.py:53
  173.4 0.7 compare_reduce_fusion
  174.1 0.6 compare_reduce_fusion.2
  177.4 10.4 %while.1 = (s32[]{:T(128)}, f32[512,512]{1,0:T(8,128)S(1)}, s32[4,2]{0,1:T(2,128)S(1)}, f32[4,128,128]{2,1,0:T(8,128)}, s32[]{:T(128)}) while((s32[]{:T(128)}, f32[512,512]{1,0:T(8,128)S(1)}, s32[4,2]{0,1:T(2,128)S(1)}, f32[4,128,128]{2,1,0:T(8,128)}, s32[]{:T(128)}) %tuple.31), condition=%wide.while_cond, body=%wide.while_body.sunk | while | flops 2 | bytes 132205 | solution.py:16
  178.1 2.0 bitcast_dynamic-update-slice_fusion.2
  180.7 2.0 bitcast_dynamic-update-slice_fusion.2
  183.2 2.0 bitcast_dynamic-update-slice_fusion.2
  185.8 2.0 bitcast_dynamic-update-slice_fusion.2
  187.8 1.0 copy-done.10
  188.8 40.1 %custom-call.33 = f32[4,128,128]{1,2,0:T(8,128)S(1)} custom-call(f32[4,128,128]{2,1,0:T(8,128)} %get-tuple-element.9), custom_call_target="InvertDiagBlocksLowerTriangular" | custom-call | tf_op jit(solution)/shard_map/triangular_solve | solution.py:16
  228.9 3.6 fusion.12
  232.5 1.9 copy.18
  234.4 5.2 %convolution_subtract_fusion.1 = f32[4096,128]{1,0:T(8,128)S(1)} fusion(f32[4096,128]{0,1:T(8,128)S(1)} %fusion.12, f32[4096,512]{1,0:T(8,128)} %scatter_fusion.1, f32[512,512]{1,0:T(8,128)} %copy-done.10), kind=kOutput, calls=%fused_computation.17 | convolution fusion | flops 805830656 | bytes 6356992 | tf_op jit(solution)/shard_map/triangular_solve | solution.py:16
  239.5 3.3 fusion.27
  242.9 3.4 copy.19
  246.2 9.4 %convolution_subtract_fusion = f32[4096,128]{1,0:T(8,128)S(1)} fusion(f32[4096,128]{0,1:T(8,128)} %fusion.27, f32[4096,128]{0,1:T(8,128)S(1)} %fusion.12, f32[4096,512]{1,0:T(8,128)} %scatter_fusion.1, f32[512,512]{1,0:T(8,128)} %copy-done.10), kind=kOutput, calls=%fused_computation.16 | convolution fusion | flops 1612185600 | bytes 8519680 | tf_op jit(solution)/shard_map/triangular_solve | solution.py:16
  255.7 2.0 fusion.26
  257.7 1.3 copy-done.9
  259.0 12.9 %fusion.6 = f32[4096,128]{1,0:T(8,128)} fusion(f32[4096,128]{0,1:T(8,128)S(1)} %fusion.26, f32[4096,128]{0,1:T(8,128)S(1)} %copy-done.8, f32[4096,128]{0,1:T(8,128)S(1)} %fusion.12, f32[4096,512]{1,0:T(8,128)} %scatter_fusion.1, f32[512,512]{1,0:T(8,128)} %copy-done.10), kind=kOutput, calls=%fused_computation.18 | convolution fusion | flops 2419589120 | bytes 10682368 | tf_op jit(solution)/shard_map/triangular_solve | solution.py:16
  271.9 2.9 copy.20
  274.8 3.5 fusion.25
  278.3 1.4 copy-done.6
  279.7 2.4 maximum_select_fusion
  282.2 1.0 slice.151
  283.1 1.0 broadcast_in_dim.35
  284.1 2.2 scatter_fusion.2
  286.3 5.8 %all-to-all-start.2 = ((f32[8,2,16,896]{3,2,1,0:T(8,128)}), f32[8,2,16,896]{3,2,1,0:T(8,128)}, u32[]{:S(2)}, u32[]{:S(2)}) async-start(f32[8,2,16,896]{3,2,1,0:T(8,128)} %bitcast.85), calls=%async_computation.2 | async-start | bytes 1835008 | tf_op jit(solution)/shard_map/all_to_all | solution.py:47
  292.1 4.0 %pad_maximum_fusion = f32[4096,512]{1,0:T(8,128)S(1)} fusion(f32[4096,128]{1,0:T(8,128)} %copy-done.6, f32[4096,128]{1,0:T(8,128)} %copy.20, f32[4096,128]{1,0:T(8,128)} %copy.19, f32[4096,128]{1,0:T(8,128)S(1)} %copy-done.2), kind=kLoop, calls=%fused_computation.8 | loop fusion | flops 6291456 | bytes 16777216 | tf_op jit(solution)/shard_map/triangular_solve | solution.py:16
  296.2 0.9 slice.149
  297.1 0.7 copy-done.4
  297.7 0.6 copy-done.5
  298.4 0.6 copy-done.7
  299.2 4.4 %maximum_bitcast_fusion = f32[1,4096,512]{2,1,0:T(8,128)} fusion(f32[3584,512]{1,0:T(8,128)S(1)} %slice.149, f32[512,512]{1,0:T(8,128)S(1)} %maximum_select_fusion.1), kind=kLoop, calls=%fused_computation.9 | loop fusion | flops 2097152 | bytes 16777216 | tf_op jit(solution)/shard_map/broadcast_in_dim | solution.py:62
  303.5 31.1 %all-gather.7.cloned.1.call-done = f32[3584,512]{1,0:T(8,128)} async-done(((f32[896,512]{1,0:T(8,128)}), f32[3584,512]{1,0:T(8,128)}) %all-gather.7.cloned.1.call-update) | async-done | bytes 7340048 | tf_op jit(solution)/shard_map/all_gather | solution.py:12
  334.7 5.4 %reduce_sum.32 = f32[896,512]{1,0:T(8,128)} reduce(f32[4,896,512]{2,1,0:T(8,128)} %bitcast.84, f32[]{:T(128)} %constant.157.clone.1), dimensions={0}, to_apply=%region_13.14 | reduce | flops 1376256 | bytes 9175044 | tf_op jit(solution)/shard_map/reduce_sum | solution.py:12
  340.1 32.9 %slice_subtract_fusion = f32[4096,896]{1,0:T(8,128)} fusion(f32[4096,1408]{1,0:T(8,128)} %bitcast.83, f32[896,512]{1,0:T(8,128)} %reduce_sum.32, f32[4096,128]{1,0:T(8,128)} %copy-done.6, f32[4096,128]{1,0:T(8,128)} %copy.20, f32[4096,128]{1,0:T(8,128)} %copy.19, f32[4096,128]{1,0:T(8,128)S(1)} %copy-done.2), kind=kOutput, calls=%fused_computation.7 | convolution fusion | flops 22558539776 | bytes 39583744 | tf_op jit(solution)/shard_map/dot_general | solution.py:56
  373.0 13.9 %scatter_fusion.3 = f32[4096,896]{1,0:T(8,128)} fusion(f32[4096,896]{1,0:T(8,128)} %slice_subtract_fusion, s32[256]{0:T(256)S(1)} %bitcast.91, f32[256,896]{1,0:T(8,128)} %bitcast.27), kind=kCustom, calls=%fused_computation.4 | custom fusion | flops 229376 | bytes 2753536 | tf_op jit(solution)/shard_map/scatter-add | solution.py:59
  (49 shorter events, 4.8 us)
Async XLA Ops:
  7.2 1.6 copy-start
  9.9 13.8 %all-to-all-start = ((s32[8,2,16]{2,1,0:T(2,128)}), s32[8,2,16]{2,1,0:T(2,128)S(1)}, u32[]{:S(2)}, u32[]{:S(2)}) async-start(s32[8,2,16]{2,1,0:T(2,128)} %bitcast.7), calls=%async_computation | async-start | bytes 16384 | tf_op jit(solution)/shard_map/all_to_all | solution.py:41
  23.7 17.2 %all-to-all-start.1 = ((f32[8,2,16,512]{3,2,1,0:T(8,128)}), f32[8,2,16,512]{3,2,1,0:T(8,128)S(1)}, u32[]{:S(2)}, u32[]{:S(2)}) async-start(f32[8,2,16,512]{3,2,1,0:T(8,128)} %bitcast.10), calls=%async_computation.1 | async-start | bytes 1048576 | tf_op jit(solution)/shard_map/all_to_all | solution.py:40
  27.2 58.7 %all-gather.5.cloned.1.call-start = ((), (), s32[]{:S(2)}) async-start(), calls=%async_computation.3 | async-start | bytes 5242880 | tf_op jit(solution)/shard_map/all_gather | solution.py:12
  52.3 282.4 %all-gather.7.cloned.1.call-start = ((), (), s32[]{:S(2)}) async-start(), calls=%async_computation.4 | async-start | bytes 9175040 | tf_op jit(solution)/shard_map/all_gather | solution.py:12
  89.3 1.0 copy-start.11
  187.8 1.0 copy-start.10
  255.7 3.3 copy-start.8
  257.7 1.3 copy-start.9
  274.8 5.0 %copy-start.2 = (f32[4096,128]{1,0:T(8,128)S(1)}, f32[4096,128]{1,0:T(8,128)}, u32[]{:S(2)}) copy-start(f32[4096,128]{1,0:T(8,128)} %copy.18) | copy-start | bytes 6291460
  274.8 5.0 %copy-start.3 = (f32[4096,128]{1,0:T(8,128)S(1)}, f32[4096,128]{1,0:T(8,128)}, u32[]{:S(2)}) copy-start(f32[4096,128]{1,0:T(8,128)} %copy.19) | copy-start | bytes 6291460
  278.3 1.4 copy-start.6
  286.3 86.7 %all-to-all-start.2 = ((f32[8,2,16,896]{3,2,1,0:T(8,128)}), f32[8,2,16,896]{3,2,1,0:T(8,128)}, u32[]{:S(2)}, u32[]{:S(2)}) async-start(f32[8,2,16,896]{3,2,1,0:T(8,128)} %bitcast.85), calls=%async_computation.2 | async-start | bytes 1835008 | tf_op jit(solution)/shard_map/all_to_all | solution.py:47
  296.1 1.6 copy-start.4
  296.1 2.2 copy-start.5
  296.2 2.8 copy-start.7
  373.0 13.9 %copy-start.1 = (s32[1,1,4,16]{3,2,1,0:T(4,128)S(1)}, s32[1,1,4,16]{3,2,1,0:T(4,128)}, u32[]{:S(2)}) copy-start(s32[1,1,4,16]{3,2,1,0:T(4,128)} %param.7) | copy-start | bytes 772
Sparse Core Ops, SparseCore 0:
  52.4 33.5 all-gather.4
  282.3 52.3 all-gather.6
